TPU v7x, 128 devices: a whole 4x4x4 slice. The times are simulated.
128 devices in a mesh: expert: 32 (over y, z, core), hidden: 4 (over x).
Axes of the slice: x: 4, y: 4, z: 4, core: 2. Of those that a mesh axis runs over, the one named last changes fastest.
Arguments:
- tokens: bfloat16 [2048, 7168], P('expert'), may hold values from -6 to 6
- expert_ids: int32 [2048, 8], replicated, may hold values from 0 to 31, all different within a row; in each aligned block of 64 rows (0 to 63, 64 to 127, ...) at most 24 rows name the same one
- gate_weight: bfloat16 [32, 7168, 2048], P('expert', None, 'hidden')
- up_weight: bfloat16 [32, 7168, 2048], P('expert', None, 'hidden')
Outputs:
- expert_hidden: bfloat16 [32, 32, 24, 2048], P('expert', None, None, 'hidden')
Inputs may be any that keep to these rules, and one draw needn't show every extreme that they name: `expert_ids`: each row names 8 different experts; among the rows of one device no expert is named more than 24 times, and in every draw some expert is named exactly 24 times there.
All inputs are finite; a program needn't handle non-finite values.
Results may differ from a plain program's by a relative error of at most 0.0058.
Values may be sent and summed in bfloat16 or wider, within the bound.
No kernel may reach another device: no remote copies, remote signals or barrier semaphores. Data moves between devices by JAX's collectives and lax.ppermute only.
A program may use at most 192 MiB of HBM per device.

v0:
```python
import jax
import jax.numpy as jnp
from jax import lax
from jax.sharding import PartitionSpec as P

TOPK = 8
EXPERTS = 32
SWEEPS = 5
TOK_DEV = 64
CAP = 24
EPS = 1e-06


def dispatch_rows(block_ids, tokens):
    tok_local, topk = block_ids.shape
    flat_ids = block_ids.reshape(-1)
    pairs = flat_ids.shape[0]
    onehot = (flat_ids[:, None] == jnp.arange(EXPERTS, dtype=jnp.int32)[None, :]).astype(
        jnp.bfloat16
    )
    earlier = (
        jnp.arange(pairs, dtype=jnp.int32)[:, None] > jnp.arange(pairs, dtype=jnp.int32)[None, :]
    ).astype(jnp.bfloat16)
    before = jnp.dot(earlier, onehot, preferred_element_type=jnp.float32)
    my_rank = jnp.sum(before * onehot.astype(jnp.float32), axis=1).astype(jnp.int32)
    pair_ids = flat_ids.reshape(tok_local, topk)
    pair_rank = my_rank.reshape(tok_local, topk)
    hit = (pair_ids[None, None] == jnp.arange(EXPERTS, dtype=jnp.int32)[:, None, None, None]) & (
        pair_rank[None, None] == jnp.arange(CAP, dtype=jnp.int32)[None, :, None, None]
    )
    select = jnp.any(hit, axis=3).astype(tokens.dtype)
    rows = jnp.einsum("est,td->esd", select, tokens, preferred_element_type=jnp.float32)
    return rows.astype(tokens.dtype)[:, None]


def hidden_sum(values):
    n = lax.axis_size("hidden")
    total = values
    for shift in range(1, n):
        total = total + lax.ppermute(values, "hidden", [(i, (i + shift) % n) for i in range(n)])
    return total


def row_terms(weight, cols_sq):
    values = weight.astype(jnp.float32)
    return jnp.sum(values * values * cols_sq[:, None, :], axis=2)


def col_terms(weight, scale_sq):
    values = weight.astype(jnp.float32)
    return jnp.sum(values * values * scale_sq[:, :, None], axis=1)


def shards(tokens, expert_ids, gate_weight, up_weight):
    exp_local = gate_weight.shape[0]
    width = gate_weight.shape[1]
    ff_local = gate_weight.shape[2]
    ff_total = ff_local * lax.axis_size("hidden")
    my_index = lax.axis_index("expert")
    tok_local = tokens.shape[0]
    block_ids = lax.dynamic_slice_in_dim(expert_ids, my_index * tok_local, tok_local, 0)
    outgoing = dispatch_rows(block_ids, tokens)
    routed = lax.all_to_all(outgoing, "expert", split_axis=0, concat_axis=1, tiled=True)

    def sweep(_, carry):
        gate_cols, up_cols, _ = carry
        partial_rows = row_terms(gate_weight, gate_cols * gate_cols) + row_terms(
            up_weight, up_cols * up_cols
        )
        row_sums = hidden_sum(partial_rows)
        row_scale = lax.rsqrt(width * row_sums / (2 * ff_total) + EPS)
        scale_sq = row_scale * row_scale
        gate_cols = lax.rsqrt(col_terms(gate_weight, scale_sq) + EPS)
        up_cols = lax.rsqrt(col_terms(up_weight, scale_sq) + EPS)
        return (gate_cols, up_cols, row_scale)

    carry = (
        jnp.ones((exp_local, ff_local), jnp.float32),
        jnp.ones((exp_local, ff_local), jnp.float32),
        jnp.ones((exp_local, width), jnp.float32),
    )
    gate_cols, up_cols, row_scale = lax.fori_loop(0, SWEEPS, sweep, carry)
    gate_eq = (
        gate_weight.astype(jnp.float32) * row_scale[:, :, None] * gate_cols[:, None, :]
    ).astype(jnp.bfloat16)
    up_eq = (up_weight.astype(jnp.float32) * row_scale[:, :, None] * up_cols[:, None, :]).astype(
        jnp.bfloat16
    )
    both_eq = lax.optimization_barrier(jnp.concatenate([gate_eq, up_eq], axis=2))
    act = jnp.einsum("ensd,edf->ensf", routed, both_eq, preferred_element_type=jnp.float32)
    gate_act = act[..., :ff_local]
    up_act = act[..., ff_local:]
    return (jax.nn.silu(gate_act) * up_act).astype(jnp.bfloat16)


def solution(mesh):
    in_specs = (P("expert", None), P(), P("expert", None, "hidden"), P("expert", None, "hidden"))
    out_specs = P("expert", None, None, "hidden")
    return jax.shard_map(shards, mesh=mesh, in_specs=in_specs, out_specs=out_specs, check_vma=False)
```

profile of v0, /device:TPU:48, one launch (start us, length us, event | category | flops | bytes accessed | tf_op | source)
XLA Modules:
  0.0 206.0 jit_solution(10485184746225352236)
XLA Ops:
  2.5 5.7 %fusion.3 = bf16[32,1,24,7168]{3,2,1,0:T(8,128)(2,1)} fusion(pred[32,24,64]{2,1,0:T(8,128)(4,1)S(1)} %and_reduce_fusion, bf16[64,7168]{1,0:T(8,128)(2,1)S(1)} %copy-done), kind=kOutput, calls=%fused_computation.16 | convolution fusion | flops 710148096 | bytes 11976704 | tf_op jit(solution)/shard_map/est,td->esd/dot_general | solution.py:32
  8.2 8.0 %all-to-all-start = ((bf16[32,1,24,7168]{3,2,1,0:T(8,128)(2,1)}), bf16[32,1,24,7168]{3,2,1,0:T(8,128)(2,1)}, u32[]{:S(2)}, u32[]{:S(2)}) async-start(bf16[32,1,24,7168]{3,2,1,0:T(8,128)(2,1)} %fusion.3), calls=%async_computation | async-start | bytes 22020096 | tf_op jit(solution)/shard_map/all_to_all | solution.py:63
  16.3 125.4 %while.16 = (s32[]{:T(128)}, f32[1,512]{1,0:T(1,128)S(1)}, f32[1,512]{1,0:T(1,128)S(1)}, f32[1,7168]{1,0:T(1,128)}, bf16[1,7168,512]{2,1,0:T(8,128)(2,1)}, /*index=5*/bf16[1,7168,512]{2,1,0:T(8,128)(2,1)}, s32[]{:T(128)}) while((s32[]{:T(128)}, f32[1,512]{1,0:T(1,128)S(1)}, f32[1,512]{1,0:T(1,128)S(1)}, f32[1,7168]{1,0:T(1,128)}, ...), condition=%wide.region_7.0_spmd, body=%wide.region_2.0_spmd.sunk | while | flops 58757120 | bytes 30077124 | solution.py:82
  16.3 9.1 %multiply_reduce_fusion.6 = (f32[7168]{0:T(1024)S(1)}, f32[7168]{0:T(1024)S(1)}) fusion(bf16[1,7168,512]{2,1,0:T(8,128)(2,1)} %get-tuple-element.169, f32[512]{0:T(512)S(1)} %bitcast.51, f32[512]{0:T(512)S(1)} %bitcast.52, bf16[1,7168,512]{2,1,0:T(8,128)(2,1)} %get-tuple-element.168), kind=kLoop, calls=%fused_computation.2.clone.1 | loop fusion | flops 29345792 | bytes 14741504 | tf_op jit(solution)/shard_map/while/body/eval_jaxpr/reduce_sum | solution.py:46
  25.4 2.8 %collective-permute-start = (f32[1,7168]{1,0:T(1,128)S(1)}, f32[1,7168]{1,0:T(1,128)S(1)}, u32[]{:S(2)}, u32[]{:S(2)}) collective-permute-start(f32[1,7168]{1,0:T(1,128)S(1)} %bitcast.43), channel_id=1, source_target_pairs={{0,3},{1,0},{2,1},{3,2},{4,7},{5,4},{6,5},{7,6},{8,11},{9,8},{10,9... | collective-permute-start | bytes 86024 | tf_op jit(solution)/shard_map/while/body/eval_jaxpr/ppermute | solution.py:40
  30.0 3.7 %collective-permute-done.1 = f32[1,7168]{1,0:T(1,128)S(1)} collective-permute-done((f32[1,7168]{1,0:T(1,128)S(1)}, f32[1,7168]{1,0:T(1,128)S(1)}, u32[]{:S(2)}, u32[]{:S(2)}) %collective-permute-start.1) | collective-permute-done | bytes 28704 | tf_op jit(solution)/shard_map/while/body/eval_jaxpr/ppermute | solution.py:40
  34.8 7.6 %multiply_reduce_fusion.7 = (f32[512]{0:T(512)S(1)}, f32[512]{0:T(512)S(1)}) fusion(bf16[1,7168,512]{2,1,0:T(8,128)(2,1)} %get-tuple-element.169, f32[7168]{0:T(1024)S(1)} %bitcast.42, bf16[1,7168,512]{2,1,0:T(8,128)(2,1)} %get-tuple-element.168), kind=kLoop, calls=%fused_computation.clone.1 | loop fusion | flops 29359104 | bytes 14712832 | tf_op jit(solution)/shard_map/while/body/eval_jaxpr/reduce_sum | solution.py:51
  42.5 9.1 %multiply_reduce_fusion.6 = (f32[7168]{0:T(1024)S(1)}, f32[7168]{0:T(1024)S(1)}) fusion(bf16[1,7168,512]{2,1,0:T(8,128)(2,1)} %get-tuple-element.169, f32[512]{0:T(512)S(1)} %bitcast.51, f32[512]{0:T(512)S(1)} %bitcast.52, bf16[1,7168,512]{2,1,0:T(8,128)(2,1)} %get-tuple-element.168), kind=kLoop, calls=%fused_computation.2.clone.1 | loop fusion | flops 29345792 | bytes 14741504 | tf_op jit(solution)/shard_map/while/body/eval_jaxpr/reduce_sum | solution.py:46
  52.0 1.4 collective-permute-start.1
  53.4 1.2 collective-permute-start.2
  55.5 1.9 collective-permute-done.1
  57.4 1.1 collective-permute-done.2
  59.2 7.6 %multiply_reduce_fusion.7 = (f32[512]{0:T(512)S(1)}, f32[512]{0:T(512)S(1)}) fusion(bf16[1,7168,512]{2,1,0:T(8,128)(2,1)} %get-tuple-element.169, f32[7168]{0:T(1024)S(1)} %bitcast.42, bf16[1,7168,512]{2,1,0:T(8,128)(2,1)} %get-tuple-element.168), kind=kLoop, calls=%fused_computation.clone.1 | loop fusion | flops 29359104 | bytes 14712832 | tf_op jit(solution)/shard_map/while/body/eval_jaxpr/reduce_sum | solution.py:51
  66.8 9.1 %multiply_reduce_fusion.6 = (f32[7168]{0:T(1024)S(1)}, f32[7168]{0:T(1024)S(1)}) fusion(bf16[1,7168,512]{2,1,0:T(8,128)(2,1)} %get-tuple-element.169, f32[512]{0:T(512)S(1)} %bitcast.51, f32[512]{0:T(512)S(1)} %bitcast.52, bf16[1,7168,512]{2,1,0:T(8,128)(2,1)} %get-tuple-element.168), kind=kLoop, calls=%fused_computation.2.clone.1 | loop fusion | flops 29345792 | bytes 14741504 | tf_op jit(solution)/shard_map/while/body/eval_jaxpr/reduce_sum | solution.py:46
  76.0 1.8 collective-permute-start
  78.7 1.2 collective-permute-done
  79.9 3.2 %collective-permute-done.1 = f32[1,7168]{1,0:T(1,128)S(1)} collective-permute-done((f32[1,7168]{1,0:T(1,128)S(1)}, f32[1,7168]{1,0:T(1,128)S(1)}, u32[]{:S(2)}, u32[]{:S(2)}) %collective-permute-start.1) | collective-permute-done | bytes 28704 | tf_op jit(solution)/shard_map/while/body/eval_jaxpr/ppermute | solution.py:40
  84.4 7.6 %multiply_reduce_fusion.7 = (f32[512]{0:T(512)S(1)}, f32[512]{0:T(512)S(1)}) fusion(bf16[1,7168,512]{2,1,0:T(8,128)(2,1)} %get-tuple-element.169, f32[7168]{0:T(1024)S(1)} %bitcast.42, bf16[1,7168,512]{2,1,0:T(8,128)(2,1)} %get-tuple-element.168), kind=kLoop, calls=%fused_computation.clone.1 | loop fusion | flops 29359104 | bytes 14712832 | tf_op jit(solution)/shard_map/while/body/eval_jaxpr/reduce_sum | solution.py:51
  92.1 9.1 %multiply_reduce_fusion.6 = (f32[7168]{0:T(1024)S(1)}, f32[7168]{0:T(1024)S(1)}) fusion(bf16[1,7168,512]{2,1,0:T(8,128)(2,1)} %get-tuple-element.169, f32[512]{0:T(512)S(1)} %bitcast.51, f32[512]{0:T(512)S(1)} %bitcast.52, bf16[1,7168,512]{2,1,0:T(8,128)(2,1)} %get-tuple-element.168), kind=kLoop, calls=%fused_computation.2.clone.1 | loop fusion | flops 29345792 | bytes 14741504 | tf_op jit(solution)/shard_map/while/body/eval_jaxpr/reduce_sum | solution.py:46
  103.0 1.1 collective-permute-start.2
  104.1 1.0 collective-permute-done
  105.2 2.3 %collective-permute-done.1 = f32[1,7168]{1,0:T(1,128)S(1)} collective-permute-done((f32[1,7168]{1,0:T(1,128)S(1)}, f32[1,7168]{1,0:T(1,128)S(1)}, u32[]{:S(2)}, u32[]{:S(2)}) %collective-permute-start.1) | collective-permute-done | bytes 28704 | tf_op jit(solution)/shard_map/while/body/eval_jaxpr/ppermute | solution.py:40
  108.8 7.6 %multiply_reduce_fusion.7 = (f32[512]{0:T(512)S(1)}, f32[512]{0:T(512)S(1)}) fusion(bf16[1,7168,512]{2,1,0:T(8,128)(2,1)} %get-tuple-element.169, f32[7168]{0:T(1024)S(1)} %bitcast.42, bf16[1,7168,512]{2,1,0:T(8,128)(2,1)} %get-tuple-element.168), kind=kLoop, calls=%fused_computation.clone.1 | loop fusion | flops 29359104 | bytes 14712832 | tf_op jit(solution)/shard_map/while/body/eval_jaxpr/reduce_sum | solution.py:51
  116.5 9.1 %multiply_reduce_fusion.6 = (f32[7168]{0:T(1024)S(1)}, f32[7168]{0:T(1024)S(1)}) fusion(bf16[1,7168,512]{2,1,0:T(8,128)(2,1)} %get-tuple-element.169, f32[512]{0:T(512)S(1)} %bitcast.51, f32[512]{0:T(512)S(1)} %bitcast.52, bf16[1,7168,512]{2,1,0:T(8,128)(2,1)} %get-tuple-element.168), kind=kLoop, calls=%fused_computation.2.clone.1 | loop fusion | flops 29345792 | bytes 14741504 | tf_op jit(solution)/shard_map/while/body/eval_jaxpr/reduce_sum | solution.py:46
  125.6 1.8 collective-permute-start
  129.5 3.2 %collective-permute-done.1 = f32[1,7168]{1,0:T(1,128)S(1)} collective-permute-done((f32[1,7168]{1,0:T(1,128)S(1)}, f32[1,7168]{1,0:T(1,128)S(1)}, u32[]{:S(2)}, u32[]{:S(2)}) %collective-permute-start.1) | collective-permute-done | bytes 28704 | tf_op jit(solution)/shard_map/while/body/eval_jaxpr/ppermute | solution.py:40
  134.1 7.6 %multiply_reduce_fusion.7 = (f32[512]{0:T(512)S(1)}, f32[512]{0:T(512)S(1)}) fusion(bf16[1,7168,512]{2,1,0:T(8,128)(2,1)} %get-tuple-element.169, f32[7168]{0:T(1024)S(1)} %bitcast.42, bf16[1,7168,512]{2,1,0:T(8,128)(2,1)} %get-tuple-element.168), kind=kLoop, calls=%fused_computation.clone.1 | loop fusion | flops 29359104 | bytes 14712832 | tf_op jit(solution)/shard_map/while/body/eval_jaxpr/reduce_sum | solution.py:51
  141.7 7.4 %multiply_convert_fusion.1 = (bf16[1,7168,512]{2,1,0:T(8,128)(2,1)S(1)}, bf16[1,7168,512]{2,1,0:T(8,128)(2,1)S(1)}) fusion(bf16[1,7168,512]{2,1,0:T(8,128)(2,1)} %get-tuple-element.171, f32[512]{0:T(512)S(1)} %bitcast.48, f32[7168]{0:T(1024)} %bitcast.53, f32[512]{0:T(512)S(1)} %bitcast.50, bf16[1,7168,512]{2,1,0:T(8,128)(2,1)} %get-tuple-element.172), kind=kLoop, calls=%fused_computation.13 | loop fusion | flops 29360128 | bytes 29392896 | tf_op jit(solution)/shard_map/convert_element_type | solution.py:85
  149.2 6.5 %pad_maximum_fusion = bf16[1,7168,1024]{2,1,0:T(8,128)(2,1)} fusion(bf16[1,7168,512]{2,1,0:T(8,128)(2,1)S(1)} %get-tuple-element.102, bf16[1,7168,512]{2,1,0:T(8,128)(2,1)S(1)} %get-tuple-element.101), kind=kLoop, calls=%fused_computation.9 | loop fusion | flops 29360128 | bytes 29360128 | tf_op jit(solution)/shard_map/concatenate | solution.py:89
  155.7 32.4 %all-to-all-done = bf16[32,1,24,7168]{3,2,1,0:T(8,128)(2,1)} async-done(((bf16[32,1,24,7168]{3,2,1,0:T(8,128)(2,1)}), bf16[32,1,24,7168]{3,2,1,0:T(8,128)(2,1)}, u32[]{:S(2)}, u32[]{:S(2)}) %all-to-all-start) | async-done | bytes 11010080 | tf_op jit(solution)/shard_map/all_to_all | solution.py:63
  188.1 16.6 %fusion.4 = f32[1,32,24,1024]{3,2,1,0:T(8,128)S(1)} fusion(bf16[1,7168,1024]{2,1,0:T(8,128)(2,1)} %pad_maximum_fusion, bf16[32,1,24,7168]{3,2,1,0:T(8,128)(2,1)} %all-to-all-done), kind=kOutput, calls=%fused_computation.18 | convolution fusion | flops 11274289152 | bytes 28835840 | tf_op jit(solution)/shard_map/ensd,edf->ensf/dot_general | solution.py:90
  204.6 1.4 fusion.9
  (63 shorter events, 16.4 us)
Async XLA Ops:
  0.0 2.5 %copy-start = (bf16[64,7168]{1,0:T(8,128)(2,1)S(1)}, bf16[64,7168]{1,0:T(8,128)(2,1)}, u32[]{:S(2)}) copy-start(bf16[64,7168]{1,0:T(8,128)(2,1)} %param.6) | copy-start | bytes 2752516
  8.2 179.9 %all-to-all-start = ((bf16[32,1,24,7168]{3,2,1,0:T(8,128)(2,1)}), bf16[32,1,24,7168]{3,2,1,0:T(8,128)(2,1)}, u32[]{:S(2)}, u32[]{:S(2)}) async-start(bf16[32,1,24,7168]{3,2,1,0:T(8,128)(2,1)} %fusion.3), calls=%async_computation | async-start | bytes 22020096 | tf_op jit(solution)/shard_map/all_to_all | solution.py:63
  25.4 4.6 %collective-permute-start = (f32[1,7168]{1,0:T(1,128)S(1)}, f32[1,7168]{1,0:T(1,128)S(1)}, u32[]{:S(2)}, u32[]{:S(2)}) collective-permute-start(f32[1,7168]{1,0:T(1,128)S(1)} %bitcast.43), channel_id=1, source_target_pairs={{0,3},{1,0},{2,1},{3,2},{4,7},{5,4},{6,5},{7,6},{8,11},{9,8},{10,9... | collective-permute-start | bytes 86024 | tf_op jit(solution)/shard_map/while/body/eval_jaxpr/ppermute | solution.py:40
  28.2 5.4 %collective-permute-start.1 = (f32[1,7168]{1,0:T(1,128)S(1)}, f32[1,7168]{1,0:T(1,128)S(1)}, u32[]{:S(2)}, u32[]{:S(2)}) collective-permute-start(f32[1,7168]{1,0:T(1,128)S(1)} %bitcast.44), channel_id=1, source_target_pairs={{0,2},{1,3},{2,0},{3,1},{4,6},{5,7},{6,4},{7,5},{8,10},{9,11},{10,... | collective-permute-start | bytes 86024 | tf_op jit(solution)/shard_map/while/body/eval_jaxpr/ppermute | solution.py:40
  29.0 5.1 %collective-permute-start.2 = (f32[1,7168]{1,0:T(1,128)S(1)}, f32[1,7168]{1,0:T(1,128)S(1)}, u32[]{:S(2)}, u32[]{:S(2)}) collective-permute-start(f32[1,7168]{1,0:T(1,128)S(1)} %bitcast.45), channel_id=1, source_target_pairs={{0,1},{1,2},{2,3},{3,0},{4,5},{5,6},{6,7},{7,4},{8,9},{9,10},{10,1... | collective-permute-start | bytes 86024 | tf_op jit(solution)/shard_map/while/body/eval_jaxpr/ppermute | solution.py:40
  51.6 3.9 %collective-permute-start = (f32[1,7168]{1,0:T(1,128)S(1)}, f32[1,7168]{1,0:T(1,128)S(1)}, u32[]{:S(2)}, u32[]{:S(2)}) collective-permute-start(f32[1,7168]{1,0:T(1,128)S(1)} %bitcast.43), channel_id=1, source_target_pairs={{0,3},{1,0},{2,1},{3,2},{4,7},{5,4},{6,5},{7,6},{8,11},{9,8},{10,9... | collective-permute-start | bytes 86024 | tf_op jit(solution)/shard_map/while/body/eval_jaxpr/ppermute | solution.py:40
  52.0 5.4 %collective-permute-start.1 = (f32[1,7168]{1,0:T(1,128)S(1)}, f32[1,7168]{1,0:T(1,128)S(1)}, u32[]{:S(2)}, u32[]{:S(2)}) collective-permute-start(f32[1,7168]{1,0:T(1,128)S(1)} %bitcast.44), channel_id=1, source_target_pairs={{0,2},{1,3},{2,0},{3,1},{4,6},{5,7},{6,4},{7,5},{8,10},{9,11},{10,... | collective-permute-start | bytes 86024 | tf_op jit(solution)/shard_map/while/body/eval_jaxpr/ppermute | solution.py:40
  53.4 5.1 %collective-permute-start.2 = (f32[1,7168]{1,0:T(1,128)S(1)}, f32[1,7168]{1,0:T(1,128)S(1)}, u32[]{:S(2)}, u32[]{:S(2)}) collective-permute-start(f32[1,7168]{1,0:T(1,128)S(1)} %bitcast.45), channel_id=1, source_target_pairs={{0,1},{1,2},{2,3},{3,0},{4,5},{5,6},{6,7},{7,4},{8,9},{9,10},{10,1... | collective-permute-start | bytes 86024 | tf_op jit(solution)/shard_map/while/body/eval_jaxpr/ppermute | solution.py:40
  76.0 3.9 %collective-permute-start = (f32[1,7168]{1,0:T(1,128)S(1)}, f32[1,7168]{1,0:T(1,128)S(1)}, u32[]{:S(2)}, u32[]{:S(2)}) collective-permute-start(f32[1,7168]{1,0:T(1,128)S(1)} %bitcast.43), channel_id=1, source_target_pairs={{0,3},{1,0},{2,1},{3,2},{4,7},{5,4},{6,5},{7,6},{8,11},{9,8},{10,9... | collective-permute-start | bytes 86024 | tf_op jit(solution)/shard_map/while/body/eval_jaxpr/ppermute | solution.py:40
  77.8 5.4 %collective-permute-start.1 = (f32[1,7168]{1,0:T(1,128)S(1)}, f32[1,7168]{1,0:T(1,128)S(1)}, u32[]{:S(2)}, u32[]{:S(2)}) collective-permute-start(f32[1,7168]{1,0:T(1,128)S(1)} %bitcast.44), channel_id=1, source_target_pairs={{0,2},{1,3},{2,0},{3,1},{4,6},{5,7},{6,4},{7,5},{8,10},{9,11},{10,... | collective-permute-start | bytes 86024 | tf_op jit(solution)/shard_map/while/body/eval_jaxpr/ppermute | solution.py:40
  78.7 5.1 %collective-permute-start.2 = (f32[1,7168]{1,0:T(1,128)S(1)}, f32[1,7168]{1,0:T(1,128)S(1)}, u32[]{:S(2)}, u32[]{:S(2)}) collective-permute-start(f32[1,7168]{1,0:T(1,128)S(1)} %bitcast.45), channel_id=1, source_target_pairs={{0,1},{1,2},{2,3},{3,0},{4,5},{5,6},{6,7},{7,4},{8,9},{9,10},{10,1... | collective-permute-start | bytes 86024 | tf_op jit(solution)/shard_map/while/body/eval_jaxpr/ppermute | solution.py:40
  101.2 3.9 %collective-permute-start = (f32[1,7168]{1,0:T(1,128)S(1)}, f32[1,7168]{1,0:T(1,128)S(1)}, u32[]{:S(2)}, u32[]{:S(2)}) collective-permute-start(f32[1,7168]{1,0:T(1,128)S(1)} %bitcast.43), channel_id=1, source_target_pairs={{0,3},{1,0},{2,1},{3,2},{4,7},{5,4},{6,5},{7,6},{8,11},{9,8},{10,9... | collective-permute-start | bytes 86024 | tf_op jit(solution)/shard_map/while/body/eval_jaxpr/ppermute | solution.py:40
  102.1 5.4 %collective-permute-start.1 = (f32[1,7168]{1,0:T(1,128)S(1)}, f32[1,7168]{1,0:T(1,128)S(1)}, u32[]{:S(2)}, u32[]{:S(2)}) collective-permute-start(f32[1,7168]{1,0:T(1,128)S(1)} %bitcast.44), channel_id=1, source_target_pairs={{0,2},{1,3},{2,0},{3,1},{4,6},{5,7},{6,4},{7,5},{8,10},{9,11},{10,... | collective-permute-start | bytes 86024 | tf_op jit(solution)/shard_map/while/body/eval_jaxpr/ppermute | solution.py:40
  103.0 5.1 %collective-permute-start.2 = (f32[1,7168]{1,0:T(1,128)S(1)}, f32[1,7168]{1,0:T(1,128)S(1)}, u32[]{:S(2)}, u32[]{:S(2)}) collective-permute-start(f32[1,7168]{1,0:T(1,128)S(1)} %bitcast.45), channel_id=1, source_target_pairs={{0,1},{1,2},{2,3},{3,0},{4,5},{5,6},{6,7},{7,4},{8,9},{9,10},{10,1... | collective-permute-start | bytes 86024 | tf_op jit(solution)/shard_map/while/body/eval_jaxpr/ppermute | solution.py:40
  125.6 3.9 %collective-permute-start = (f32[1,7168]{1,0:T(1,128)S(1)}, f32[1,7168]{1,0:T(1,128)S(1)}, u32[]{:S(2)}, u32[]{:S(2)}) collective-permute-start(f32[1,7168]{1,0:T(1,128)S(1)} %bitcast.43), channel_id=1, source_target_pairs={{0,3},{1,0},{2,1},{3,2},{4,7},{5,4},{6,5},{7,6},{8,11},{9,8},{10,9... | collective-permute-start | bytes 86024 | tf_op jit(solution)/shard_map/while/body/eval_jaxpr/ppermute | solution.py:40
  127.4 5.4 %collective-permute-start.1 = (f32[1,7168]{1,0:T(1,128)S(1)}, f32[1,7168]{1,0:T(1,128)S(1)}, u32[]{:S(2)}, u32[]{:S(2)}) collective-permute-start(f32[1,7168]{1,0:T(1,128)S(1)} %bitcast.44), channel_id=1, source_target_pairs={{0,2},{1,3},{2,0},{3,1},{4,6},{5,7},{6,4},{7,5},{8,10},{9,11},{10,... | collective-permute-start | bytes 86024 | tf_op jit(solution)/shard_map/while/body/eval_jaxpr/ppermute | solution.py:40
  128.3 5.1 %collective-permute-start.2 = (f32[1,7168]{1,0:T(1,128)S(1)}, f32[1,7168]{1,0:T(1,128)S(1)}, u32[]{:S(2)}, u32[]{:S(2)}) collective-permute-start(f32[1,7168]{1,0:T(1,128)S(1)} %bitcast.45), channel_id=1, source_target_pairs={{0,1},{1,2},{2,3},{3,0},{4,5},{5,6},{6,7},{7,4},{8,9},{9,10},{10,1... | collective-permute-start | bytes 86024 | tf_op jit(solution)/shard_map/while/body/eval_jaxpr/ppermute | solution.py:40
  188.1 18.0 %copy-start.1 = (bf16[64,7168]{1,0:T(8,128)(2,1)S(1)}, bf16[64,7168]{1,0:T(8,128)(2,1)}, u32[]{:S(2)}) copy-start(bf16[64,7168]{1,0:T(8,128)(2,1)} %param.6) | copy-start | bytes 2752516
where the time goes:
time: 206 us
  other arithmetic  103 us (50%)
  waiting for transfers between devices  54.4 us (26%)
  starting transfers between devices  24.1 us (12%)
  matrix products  22.5 us (11%)
    reduce_sum x5, other arithmetic, row_terms(): return jnp.sum(values * values * cols_sq[:, None, :], axis=2)  45.5 us
    reduce_sum x5, other arithmetic, col_terms(): return jnp.sum(values * values * scale_sq[:, :, None], axis=1)  37.9 us
    all_to_all x1, waiting for transfers between devices, shards(): lax.all_to_all(outgoing, 'expert', split_axis=0, concat_axis=1, tiled=True)  32.4 us
    ppermute x15, waiting for transfers between devices, hidden_sum(): lax.ppermute(values, 'hidden', [(i, (i + shift) % n) for i in range(n)])  22 us
    dot_general x1, matrix products, shards(): jnp.einsum('ensd,edf->ensf', routed, both_eq, preferred_element_type=jnp....  16.6 us
    ppermute x15, starting transfers between devices, hidden_sum(): lax.ppermute(values, 'hidden', [(i, (i + shift) % n) for i in range(n)])  16.1 us
    all_to_all x1, starting transfers between devices, shards(): lax.all_to_all(outgoing, 'expert', split_axis=0, concat_axis=1, tiled=True)  8.04 us
    convert_element_type x1, other arithmetic, shards(): gate_eq = (gate_weight.astype(jnp.float32) * row_scale[:, :, None] * gate...  7.45 us
  transfers between devices with their start and end apart: 16, of which 15 were waited for; matrix products, arithmetic and copies ran while one was open for 49% of the time, Pallas kernels for 0%

commit v1 on v0

--- a/solution.py
+++ b/solution.py
@@ -60,7 +60,12 @@
     tok_local = tokens.shape[0]
     block_ids = lax.dynamic_slice_in_dim(expert_ids, my_index * tok_local, tok_local, 0)
     outgoing = dispatch_rows(block_ids, tokens)
-    routed = lax.all_to_all(outgoing, "expert", split_axis=0, concat_axis=1, tiled=True)
+    routed = jnp.concatenate(
+        lax.all_to_all(
+            jnp.stack(jnp.split(outgoing, lax.axis_size("expert"), axis=0)), "expert", 0, 0
+        ),
+        axis=1,
+    )
 
     def sweep(_, carry):
         gate_cols, up_cols, _ = carry

time: 206 us -> 228 us (1.11)
  local copies, waits for them, and re-layouts: 1.17 us -> 25.6 us
  starting transfers between devices: 24.1 us -> 30.6 us
  waiting for transfers between devices: 54.4 us -> 47.9 us
  matrix products: 22.5 us -> 20 us
    unnamed x4 -> x35, local copies, waits for them, and re-layouts: 0.01 us -> 23.7 us
    ppermute x15, waiting for transfers between devices: 22 us -> 15 us  [hidden_sum(): lax.ppermute(values, 'hidden', [(i, (i + shift) % n) for i in range(n)])]
    ppermute x15, starting transfers between devices: 16.1 us -> 22.6 us  [hidden_sum(): lax.ppermute(values, 'hidden', [(i, (i + shift) % n) for i in range(n)])]
    dot_general x1, matrix products: 5.66 us -> 3.16 us  [dispatch_rows(): jnp.einsum('est,td->esd', select, tokens, preferred_element_type=jnp.floa...]
  transfers between devices with their start and end apart: 16 -> 16, of which waited for: 15 -> 15; matrix products, arithmetic and copies ran while one was open for 49% -> 44% of each run, Pallas kernels for 0% -> 0%
where the time goes in v1:
time: 228 us
  other arithmetic  103 us (45%)
  waiting for transfers between devices  47.9 us (21%)
  starting transfers between devices  30.6 us (13%)
  local copies, waits for them, and re-layouts  25.6 us (11%)
  matrix products  20 us (9%)
    reduce_sum x5, other arithmetic, row_terms(): return jnp.sum(values * values * cols_sq[:, None, :], axis=2)  45.5 us
    reduce_sum x5, other arithmetic, col_terms(): return jnp.sum(values * values * scale_sq[:, :, None], axis=1)  37.9 us
    all_to_all x1, waiting for transfers between devices, shards(): lax.all_to_all(jnp.stack(jnp.split(outgoing, lax.axis_size('expert'), axi...  32.9 us
    unnamed x35, local copies, waits for them, and re-layouts  23.7 us
    ppermute x15, starting transfers between devices, hidden_sum(): lax.ppermute(values, 'hidden', [(i, (i + shift) % n) for i in range(n)])  22.6 us
    dot_general x1, matrix products, shards(): jnp.einsum('ensd,edf->ensf', routed, both_eq, preferred_element_type=jnp....  16.6 us
    ppermute x15, waiting for transfers between devices, hidden_sum(): lax.ppermute(values, 'hidden', [(i, (i + shift) % n) for i in range(n)])  15 us
    all_to_all x1, starting transfers between devices, shards(): lax.all_to_all(jnp.stack(jnp.split(outgoing, lax.axis_size('expert'), axi...  8.04 us
  transfers between devices with their start and end apart: 16, of which 15 were waited for; matrix products, arithmetic and copies ran while one was open for 44% of the time, Pallas kernels for 0%

profile of v1, /device:TPU:48, one launch (start us, length us, event | category | flops | bytes accessed | tf_op | source)
XLA Modules:
  0.0 228.0 jit_solution(13144640175269746402)
XLA Ops:
  2.5 3.2 %convolution_convert_fusion = bf16[32,24,7168]{2,1,0:T(8,128)(2,1)S(1)} fusion(pred[32,24,64]{2,1,0:T(8,128)(4,1)S(1)} %and_reduce_fusion, bf16[64,7168]{1,0:T(8,128)(2,1)S(1)} %copy-done), kind=kOutput, calls=%fused_computation.14 | convolution fusion | flops 710148096 | bytes 11976704 | tf_op jit(solution)/shard_map/est,td->esd/dot_general | solution.py:32
  30.1 8.0 %all-to-all-start = ((bf16[32,1,1,24,7168]{4,3,2,1,0:T(8,128)(2,1)}), bf16[32,1,1,24,7168]{4,3,2,1,0:T(8,128)(2,1)}, u32[]{:S(2)}, u32[]{:S(2)}) async-start(bf16[32,1,1,24,7168]{4,3,2,1,0:T(8,128)(2,1)} %fusion.11), calls=%async_computation | async-start | bytes 22020096 | tf_op jit(solution)/shard_map/all_to_all | solution.py:64
  38.2 124.9 %while.16 = (s32[]{:T(128)}, f32[1,512]{1,0:T(1,128)S(1)}, f32[1,512]{1,0:T(1,128)S(1)}, f32[1,7168]{1,0:T(1,128)}, bf16[1,7168,512]{2,1,0:T(8,128)(2,1)}, /*index=5*/bf16[1,7168,512]{2,1,0:T(8,128)(2,1)}, s32[]{:T(128)}) while((s32[]{:T(128)}, f32[1,512]{1,0:T(1,128)S(1)}, f32[1,512]{1,0:T(1,128)S(1)}, f32[1,7168]{1,0:T(1,128)}, ...), condition=%wide.region_7.0_spmd, body=%wide.region_2.0_spmd.sunk | while | flops 58757120 | bytes 30077124 | solution.py:87
  38.2 9.1 %multiply_reduce_fusion.6 = (f32[7168]{0:T(1024)S(1)}, f32[7168]{0:T(1024)S(1)}) fusion(bf16[1,7168,512]{2,1,0:T(8,128)(2,1)} %get-tuple-element.169, f32[512]{0:T(512)S(1)} %bitcast.175, f32[512]{0:T(512)S(1)} %bitcast.176, bf16[1,7168,512]{2,1,0:T(8,128)(2,1)} %get-tuple-element.168), kind=kLoop, calls=%fused_computation.2.clone.1 | loop fusion | flops 29345792 | bytes 14741504 | tf_op jit(solution)/shard_map/while/body/eval_jaxpr/reduce_sum | solution.py:46
  47.4 1.6 collective-permute-start.2
  48.9 2.7 %collective-permute-start.1 = (f32[1,7168]{1,0:T(1,128)S(1)}, f32[1,7168]{1,0:T(1,128)S(1)}, u32[]{:S(2)}, u32[]{:S(2)}) collective-permute-start(f32[1,7168]{1,0:T(1,128)S(1)} %bitcast.168), channel_id=1, source_target_pairs={{0,2},{1,3},{2,0},{3,1},{4,6},{5,7},{6,4},{7,5},{8,10},{9,11},{10,... | collective-permute-start | bytes 86024 | tf_op jit(solution)/shard_map/while/body/eval_jaxpr/ppermute | solution.py:40
  51.7 1.4 collective-permute-start
  54.3 1.2 collective-permute-done
  56.2 7.6 %multiply_reduce_fusion.7 = (f32[512]{0:T(512)S(1)}, f32[512]{0:T(512)S(1)}) fusion(bf16[1,7168,512]{2,1,0:T(8,128)(2,1)} %get-tuple-element.169, f32[7168]{0:T(1024)S(1)} %bitcast.166, bf16[1,7168,512]{2,1,0:T(8,128)(2,1)} %get-tuple-element.168), kind=kLoop, calls=%fused_computation.clone.1 | loop fusion | flops 29359104 | bytes 14712832 | tf_op jit(solution)/shard_map/while/body/eval_jaxpr/reduce_sum | solution.py:51
  63.9 9.1 %multiply_reduce_fusion.6 = (f32[7168]{0:T(1024)S(1)}, f32[7168]{0:T(1024)S(1)}) fusion(bf16[1,7168,512]{2,1,0:T(8,128)(2,1)} %get-tuple-element.169, f32[512]{0:T(512)S(1)} %bitcast.175, f32[512]{0:T(512)S(1)} %bitcast.176, bf16[1,7168,512]{2,1,0:T(8,128)(2,1)} %get-tuple-element.168), kind=kLoop, calls=%fused_computation.2.clone.1 | loop fusion | flops 29345792 | bytes 14741504 | tf_op jit(solution)/shard_map/while/body/eval_jaxpr/reduce_sum | solution.py:46
  73.3 3.8 %collective-permute-start.1 = (f32[1,7168]{1,0:T(1,128)S(1)}, f32[1,7168]{1,0:T(1,128)S(1)}, u32[]{:S(2)}, u32[]{:S(2)}) collective-permute-start(f32[1,7168]{1,0:T(1,128)S(1)} %bitcast.168), channel_id=1, source_target_pairs={{0,2},{1,3},{2,0},{3,1},{4,6},{5,7},{6,4},{7,5},{8,10},{9,11},{10,... | collective-permute-start | bytes 86024 | tf_op jit(solution)/shard_map/while/body/eval_jaxpr/ppermute | solution.py:40
  79.3 1.7 collective-permute-done
  81.7 7.6 %multiply_reduce_fusion.7 = (f32[512]{0:T(512)S(1)}, f32[512]{0:T(512)S(1)}) fusion(bf16[1,7168,512]{2,1,0:T(8,128)(2,1)} %get-tuple-element.169, f32[7168]{0:T(1024)S(1)} %bitcast.166, bf16[1,7168,512]{2,1,0:T(8,128)(2,1)} %get-tuple-element.168), kind=kLoop, calls=%fused_computation.clone.1 | loop fusion | flops 29359104 | bytes 14712832 | tf_op jit(solution)/shard_map/while/body/eval_jaxpr/reduce_sum | solution.py:51
  89.4 9.1 %multiply_reduce_fusion.6 = (f32[7168]{0:T(1024)S(1)}, f32[7168]{0:T(1024)S(1)}) fusion(bf16[1,7168,512]{2,1,0:T(8,128)(2,1)} %get-tuple-element.169, f32[512]{0:T(512)S(1)} %bitcast.175, f32[512]{0:T(512)S(1)} %bitcast.176, bf16[1,7168,512]{2,1,0:T(8,128)(2,1)} %get-tuple-element.168), kind=kLoop, calls=%fused_computation.2.clone.1 | loop fusion | flops 29345792 | bytes 14741504 | tf_op jit(solution)/shard_map/while/body/eval_jaxpr/reduce_sum | solution.py:46
  98.6 2.7 %collective-permute-start.1 = (f32[1,7168]{1,0:T(1,128)S(1)}, f32[1,7168]{1,0:T(1,128)S(1)}, u32[]{:S(2)}, u32[]{:S(2)}) collective-permute-start(f32[1,7168]{1,0:T(1,128)S(1)} %bitcast.168), channel_id=1, source_target_pairs={{0,2},{1,3},{2,0},{3,1},{4,6},{5,7},{6,4},{7,5},{8,10},{9,11},{10,... | collective-permute-start | bytes 86024 | tf_op jit(solution)/shard_map/while/body/eval_jaxpr/ppermute | solution.py:40
  101.3 1.4 collective-permute-start
  105.8 7.6 %multiply_reduce_fusion.7 = (f32[512]{0:T(512)S(1)}, f32[512]{0:T(512)S(1)}) fusion(bf16[1,7168,512]{2,1,0:T(8,128)(2,1)} %get-tuple-element.169, f32[7168]{0:T(1024)S(1)} %bitcast.166, bf16[1,7168,512]{2,1,0:T(8,128)(2,1)} %get-tuple-element.168), kind=kLoop, calls=%fused_computation.clone.1 | loop fusion | flops 29359104 | bytes 14712832 | tf_op jit(solution)/shard_map/while/body/eval_jaxpr/reduce_sum | solution.py:51
  113.5 9.1 %multiply_reduce_fusion.6 = (f32[7168]{0:T(1024)S(1)}, f32[7168]{0:T(1024)S(1)}) fusion(bf16[1,7168,512]{2,1,0:T(8,128)(2,1)} %get-tuple-element.169, f32[512]{0:T(512)S(1)} %bitcast.175, f32[512]{0:T(512)S(1)} %bitcast.176, bf16[1,7168,512]{2,1,0:T(8,128)(2,1)} %get-tuple-element.168), kind=kLoop, calls=%fused_computation.2.clone.1 | loop fusion | flops 29345792 | bytes 14741504 | tf_op jit(solution)/shard_map/while/body/eval_jaxpr/reduce_sum | solution.py:46
  122.6 1.5 collective-permute-start.2
  124.1 2.7 %collective-permute-start.1 = (f32[1,7168]{1,0:T(1,128)S(1)}, f32[1,7168]{1,0:T(1,128)S(1)}, u32[]{:S(2)}, u32[]{:S(2)}) collective-permute-start(f32[1,7168]{1,0:T(1,128)S(1)} %bitcast.168), channel_id=1, source_target_pairs={{0,2},{1,3},{2,0},{3,1},{4,6},{5,7},{6,4},{7,5},{8,10},{9,11},{10,... | collective-permute-start | bytes 86024 | tf_op jit(solution)/shard_map/while/body/eval_jaxpr/ppermute | solution.py:40
  127.8 1.7 collective-permute-done.1
  129.5 1.2 collective-permute-done
  131.4 7.6 %multiply_reduce_fusion.7 = (f32[512]{0:T(512)S(1)}, f32[512]{0:T(512)S(1)}) fusion(bf16[1,7168,512]{2,1,0:T(8,128)(2,1)} %get-tuple-element.169, f32[7168]{0:T(1024)S(1)} %bitcast.166, bf16[1,7168,512]{2,1,0:T(8,128)(2,1)} %get-tuple-element.168), kind=kLoop, calls=%fused_computation.clone.1 | loop fusion | flops 29359104 | bytes 14712832 | tf_op jit(solution)/shard_map/while/body/eval_jaxpr/reduce_sum | solution.py:51
  139.0 9.1 %multiply_reduce_fusion.6 = (f32[7168]{0:T(1024)S(1)}, f32[7168]{0:T(1024)S(1)}) fusion(bf16[1,7168,512]{2,1,0:T(8,128)(2,1)} %get-tuple-element.169, f32[512]{0:T(512)S(1)} %bitcast.175, f32[512]{0:T(512)S(1)} %bitcast.176, bf16[1,7168,512]{2,1,0:T(8,128)(2,1)} %get-tuple-element.168), kind=kLoop, calls=%fused_computation.2.clone.1 | loop fusion | flops 29345792 | bytes 14741504 | tf_op jit(solution)/shard_map/while/body/eval_jaxpr/reduce_sum | solution.py:46
  148.2 2.7 %collective-permute-start.1 = (f32[1,7168]{1,0:T(1,128)S(1)}, f32[1,7168]{1,0:T(1,128)S(1)}, u32[]{:S(2)}, u32[]{:S(2)}) collective-permute-start(f32[1,7168]{1,0:T(1,128)S(1)} %bitcast.168), channel_id=1, source_target_pairs={{0,2},{1,3},{2,0},{3,1},{4,6},{5,7},{6,4},{7,5},{8,10},{9,11},{10,... | collective-permute-start | bytes 86024 | tf_op jit(solution)/shard_map/while/body/eval_jaxpr/ppermute | solution.py:40
  150.9 1.4 collective-permute-start
  155.5 7.6 %multiply_reduce_fusion.7 = (f32[512]{0:T(512)S(1)}, f32[512]{0:T(512)S(1)}) fusion(bf16[1,7168,512]{2,1,0:T(8,128)(2,1)} %get-tuple-element.169, f32[7168]{0:T(1024)S(1)} %bitcast.166, bf16[1,7168,512]{2,1,0:T(8,128)(2,1)} %get-tuple-element.168), kind=kLoop, calls=%fused_computation.clone.1 | loop fusion | flops 29359104 | bytes 14712832 | tf_op jit(solution)/shard_map/while/body/eval_jaxpr/reduce_sum | solution.py:51
  163.1 7.5 %multiply_convert_fusion.1 = (bf16[1,7168,512]{2,1,0:T(8,128)(2,1)S(1)}, bf16[1,7168,512]{2,1,0:T(8,128)(2,1)S(1)}) fusion(bf16[1,7168,512]{2,1,0:T(8,128)(2,1)} %get-tuple-element.171, f32[512]{0:T(512)S(1)} %bitcast.174, f32[7168]{0:T(1024)} %bitcast.177, f32[512]{0:T(512)S(1)} %bitcast.172, bf16[1,7168,512]{2,1,0:T(8,128)(2,1)} %get-tuple-element.172), kind=kLoop, calls=%fused_computation.13 | loop fusion | flops 29360128 | bytes 29392896 | tf_op jit(solution)/shard_map/convert_element_type | solution.py:90
  170.6 6.5 %pad_maximum_fusion = bf16[1,7168,1024]{2,1,0:T(8,128)(2,1)} fusion(bf16[1,7168,512]{2,1,0:T(8,128)(2,1)S(1)} %get-tuple-element.102, bf16[1,7168,512]{2,1,0:T(8,128)(2,1)S(1)} %get-tuple-element.101), kind=kLoop, calls=%fused_computation.9 | loop fusion | flops 29360128 | bytes 29360128 | tf_op jit(solution)/shard_map/concatenate | solution.py:94
  177.1 32.9 %all-to-all-done = bf16[32,1,1,24,7168]{4,3,2,1,0:T(8,128)(2,1)} async-done(((bf16[32,1,1,24,7168]{4,3,2,1,0:T(8,128)(2,1)}), bf16[32,1,1,24,7168]{4,3,2,1,0:T(8,128)(2,1)}, u32[]{:S(2)}, u32[]{:S(2)}) %all-to-all-start) | async-done | bytes 11010080 | tf_op jit(solution)/shard_map/all_to_all | solution.py:64
  210.0 16.6 %fusion.3 = f32[1,32,24,1024]{3,2,1,0:T(8,128)S(1)} fusion(bf16[1,7168,1024]{2,1,0:T(8,128)(2,1)} %pad_maximum_fusion, bf16[32,1,1,24,7168]{4,3,2,1,0:T(8,128)(2,1)} %all-to-all-done), kind=kOutput, calls=%fused_computation.17 | convolution fusion | flops 11274289152 | bytes 28835840 | tf_op jit(solution)/shard_map/ensd,edf->ensf/dot_general | solution.py:95
  226.6 1.4 fusion.8
  (95 shorter events, 40.2 us)
Async XLA Ops:
  0.0 2.5 %copy-start = (bf16[64,7168]{1,0:T(8,128)(2,1)S(1)}, bf16[64,7168]{1,0:T(8,128)(2,1)}, u32[]{:S(2)}) copy-start(bf16[64,7168]{1,0:T(8,128)(2,1)} %param.6) | copy-start | bytes 2752516
  30.1 179.9 %all-to-all-start = ((bf16[32,1,1,24,7168]{4,3,2,1,0:T(8,128)(2,1)}), bf16[32,1,1,24,7168]{4,3,2,1,0:T(8,128)(2,1)}, u32[]{:S(2)}, u32[]{:S(2)}) async-start(bf16[32,1,1,24,7168]{4,3,2,1,0:T(8,128)(2,1)} %fusion.11), calls=%async_computation | async-start | bytes 22020096 | tf_op jit(solution)/shard_map/all_to_all | solution.py:64
  47.4 5.7 %collective-permute-start.2 = (f32[1,7168]{1,0:T(1,128)S(1)}, f32[1,7168]{1,0:T(1,128)S(1)}, u32[]{:S(2)}, u32[]{:S(2)}) collective-permute-start(f32[1,7168]{1,0:T(1,128)S(1)} %bitcast.167), channel_id=1, source_target_pairs={{0,1},{1,2},{2,3},{3,0},{4,5},{5,6},{6,7},{7,4},{8,9},{9,10},{10,1... | collective-permute-start | bytes 86024 | tf_op jit(solution)/shard_map/while/body/eval_jaxpr/ppermute | solution.py:40
  48.9 5.4 %collective-permute-start.1 = (f32[1,7168]{1,0:T(1,128)S(1)}, f32[1,7168]{1,0:T(1,128)S(1)}, u32[]{:S(2)}, u32[]{:S(2)}) collective-permute-start(f32[1,7168]{1,0:T(1,128)S(1)} %bitcast.168), channel_id=1, source_target_pairs={{0,2},{1,3},{2,0},{3,1},{4,6},{5,7},{6,4},{7,5},{8,10},{9,11},{10,... | collective-permute-start | bytes 86024 | tf_op jit(solution)/shard_map/while/body/eval_jaxpr/ppermute | solution.py:40
  51.7 3.9 %collective-permute-start = (f32[1,7168]{1,0:T(1,128)S(1)}, f32[1,7168]{1,0:T(1,128)S(1)}, u32[]{:S(2)}, u32[]{:S(2)}) collective-permute-start(f32[1,7168]{1,0:T(1,128)S(1)} %bitcast.169), channel_id=1, source_target_pairs={{0,3},{1,0},{2,1},{3,2},{4,7},{5,4},{6,5},{7,6},{8,11},{9,8},{10,9... | collective-permute-start | bytes 86024 | tf_op jit(solution)/shard_map/while/body/eval_jaxpr/ppermute | solution.py:40
  73.0 5.1 %collective-permute-start.2 = (f32[1,7168]{1,0:T(1,128)S(1)}, f32[1,7168]{1,0:T(1,128)S(1)}, u32[]{:S(2)}, u32[]{:S(2)}) collective-permute-start(f32[1,7168]{1,0:T(1,128)S(1)} %bitcast.167), channel_id=1, source_target_pairs={{0,1},{1,2},{2,3},{3,0},{4,5},{5,6},{6,7},{7,4},{8,9},{9,10},{10,1... | collective-permute-start | bytes 86024 | tf_op jit(solution)/shard_map/while/body/eval_jaxpr/ppermute | solution.py:40
  73.3 6.0 %collective-permute-start.1 = (f32[1,7168]{1,0:T(1,128)S(1)}, f32[1,7168]{1,0:T(1,128)S(1)}, u32[]{:S(2)}, u32[]{:S(2)}) collective-permute-start(f32[1,7168]{1,0:T(1,128)S(1)} %bitcast.168), channel_id=1, source_target_pairs={{0,2},{1,3},{2,0},{3,1},{4,6},{5,7},{6,4},{7,5},{8,10},{9,11},{10,... | collective-permute-start | bytes 86024 | tf_op jit(solution)/shard_map/while/body/eval_jaxpr/ppermute | solution.py:40
  77.2 3.9 %collective-permute-start = (f32[1,7168]{1,0:T(1,128)S(1)}, f32[1,7168]{1,0:T(1,128)S(1)}, u32[]{:S(2)}, u32[]{:S(2)}) collective-permute-start(f32[1,7168]{1,0:T(1,128)S(1)} %bitcast.169), channel_id=1, source_target_pairs={{0,3},{1,0},{2,1},{3,2},{4,7},{5,4},{6,5},{7,6},{8,11},{9,8},{10,9... | collective-permute-start | bytes 86024 | tf_op jit(solution)/shard_map/while/body/eval_jaxpr/ppermute | solution.py:40
  98.5 5.1 %collective-permute-start.2 = (f32[1,7168]{1,0:T(1,128)S(1)}, f32[1,7168]{1,0:T(1,128)S(1)}, u32[]{:S(2)}, u32[]{:S(2)}) collective-permute-start(f32[1,7168]{1,0:T(1,128)S(1)} %bitcast.167), channel_id=1, source_target_pairs={{0,1},{1,2},{2,3},{3,0},{4,5},{5,6},{6,7},{7,4},{8,9},{9,10},{10,1... | collective-permute-start | bytes 86024 | tf_op jit(solution)/shard_map/while/body/eval_jaxpr/ppermute | solution.py:40
  98.6 5.5 %collective-permute-start.1 = (f32[1,7168]{1,0:T(1,128)S(1)}, f32[1,7168]{1,0:T(1,128)S(1)}, u32[]{:S(2)}, u32[]{:S(2)}) collective-permute-start(f32[1,7168]{1,0:T(1,128)S(1)} %bitcast.168), channel_id=1, source_target_pairs={{0,2},{1,3},{2,0},{3,1},{4,6},{5,7},{6,4},{7,5},{8,10},{9,11},{10,... | collective-permute-start | bytes 86024 | tf_op jit(solution)/shard_map/while/body/eval_jaxpr/ppermute | solution.py:40
  101.3 3.9 %collective-permute-start = (f32[1,7168]{1,0:T(1,128)S(1)}, f32[1,7168]{1,0:T(1,128)S(1)}, u32[]{:S(2)}, u32[]{:S(2)}) collective-permute-start(f32[1,7168]{1,0:T(1,128)S(1)} %bitcast.169), channel_id=1, source_target_pairs={{0,3},{1,0},{2,1},{3,2},{4,7},{5,4},{6,5},{7,6},{8,11},{9,8},{10,9... | collective-permute-start | bytes 86024 | tf_op jit(solution)/shard_map/while/body/eval_jaxpr/ppermute | solution.py:40
  122.6 5.1 %collective-permute-start.2 = (f32[1,7168]{1,0:T(1,128)S(1)}, f32[1,7168]{1,0:T(1,128)S(1)}, u32[]{:S(2)}, u32[]{:S(2)}) collective-permute-start(f32[1,7168]{1,0:T(1,128)S(1)} %bitcast.167), channel_id=1, source_target_pairs={{0,1},{1,2},{2,3},{3,0},{4,5},{5,6},{6,7},{7,4},{8,9},{9,10},{10,1... | collective-permute-start | bytes 86024 | tf_op jit(solution)/shard_map/while/body/eval_jaxpr/ppermute | solution.py:40
  124.1 5.4 %collective-permute-start.1 = (f32[1,7168]{1,0:T(1,128)S(1)}, f32[1,7168]{1,0:T(1,128)S(1)}, u32[]{:S(2)}, u32[]{:S(2)}) collective-permute-start(f32[1,7168]{1,0:T(1,128)S(1)} %bitcast.168), channel_id=1, source_target_pairs={{0,2},{1,3},{2,0},{3,1},{4,6},{5,7},{6,4},{7,5},{8,10},{9,11},{10,... | collective-permute-start | bytes 86024 | tf_op jit(solution)/shard_map/while/body/eval_jaxpr/ppermute | solution.py:40
  126.8 3.9 %collective-permute-start = (f32[1,7168]{1,0:T(1,128)S(1)}, f32[1,7168]{1,0:T(1,128)S(1)}, u32[]{:S(2)}, u32[]{:S(2)}) collective-permute-start(f32[1,7168]{1,0:T(1,128)S(1)} %bitcast.169), channel_id=1, source_target_pairs={{0,3},{1,0},{2,1},{3,2},{4,7},{5,4},{6,5},{7,6},{8,11},{9,8},{10,9... | collective-permute-start | bytes 86024 | tf_op jit(solution)/shard_map/while/body/eval_jaxpr/ppermute | solution.py:40
  148.1 5.1 %collective-permute-start.2 = (f32[1,7168]{1,0:T(1,128)S(1)}, f32[1,7168]{1,0:T(1,128)S(1)}, u32[]{:S(2)}, u32[]{:S(2)}) collective-permute-start(f32[1,7168]{1,0:T(1,128)S(1)} %bitcast.167), channel_id=1, source_target_pairs={{0,1},{1,2},{2,3},{3,0},{4,5},{5,6},{6,7},{7,4},{8,9},{9,10},{10,1... | collective-permute-start | bytes 86024 | tf_op jit(solution)/shard_map/while/body/eval_jaxpr/ppermute | solution.py:40
  148.2 5.5 %collective-permute-start.1 = (f32[1,7168]{1,0:T(1,128)S(1)}, f32[1,7168]{1,0:T(1,128)S(1)}, u32[]{:S(2)}, u32[]{:S(2)}) collective-permute-start(f32[1,7168]{1,0:T(1,128)S(1)} %bitcast.168), channel_id=1, source_target_pairs={{0,2},{1,3},{2,0},{3,1},{4,6},{5,7},{6,4},{7,5},{8,10},{9,11},{10,... | collective-permute-start | bytes 86024 | tf_op jit(solution)/shard_map/while/body/eval_jaxpr/ppermute | solution.py:40
  150.9 3.9 %collective-permute-start = (f32[1,7168]{1,0:T(1,128)S(1)}, f32[1,7168]{1,0:T(1,128)S(1)}, u32[]{:S(2)}, u32[]{:S(2)}) collective-permute-start(f32[1,7168]{1,0:T(1,128)S(1)} %bitcast.169), channel_id=1, source_target_pairs={{0,3},{1,0},{2,1},{3,2},{4,7},{5,4},{6,5},{7,6},{8,11},{9,8},{10,9... | collective-permute-start | bytes 86024 | tf_op jit(solution)/shard_map/while/body/eval_jaxpr/ppermute | solution.py:40
  210.0 18.0 %copy-start.1 = (bf16[64,7168]{1,0:T(8,128)(2,1)S(1)}, bf16[64,7168]{1,0:T(8,128)(2,1)}, u32[]{:S(2)}) copy-start(bf16[64,7168]{1,0:T(8,128)(2,1)} %param.6) | copy-start | bytes 2752516
